TPU v7x, 32 devices: a whole 2x2x4 slice. The times are simulated.
32 devices in a mesh: group: 2 (over x), strip: 16 (over z, y, core).
Axes of the slice: x: 2, y: 2, z: 4, core: 2. Of those that a mesh axis runs over, the one named last changes fastest.
Arguments:
- strip_fields: float32 [3, 64, 128, 128], P(None, ('group', 'strip')), may hold values from -18 to 18
- strip_riser: int32 [64, 1], P('group'), may hold values from 0 to 3; in each aligned block of 2 rows (0 to 1, 2 to 3, ...) at most 2 rows name the same one
- strip_node: int32 [64], P('group'), may hold values from 0 to 1023
- riser_owner: int32 [2, 4], P('group'), may hold values from 0 to 15, as said below
- pivot_inv: float32 [32, 8, 128, 128], P(('group', 'strip')), may hold values from -0.2 to 1
- lower_block: float32 [32, 7, 128, 128], P(('group', 'strip')), may hold values from -0.109375 to 0.109375
- upper_block: float32 [32, 7, 128, 128], P(('group', 'strip')), may hold values from -0.109375 to 0.109375
Outputs:
- vorticity: float32 [64, 128, 128], P(('group', 'strip'))
- displacement: float32 [32, 16, 1024], P(('group', 'strip'))
Inputs may be any that keep to these rules, and one draw needn't show every extreme that they name: `strip_riser`: in each aligned block of 2 strips (the strips of one device) no riser is named more than 2 times, and some block names one riser exactly 2 times. `riser_owner`: the 4 owners in a row are distinct devices.
All inputs are finite; a program needn't handle non-finite values.
Results may differ from a plain program's by a relative error of at most 0.0003.
Values sent between devices are 32-bit elements; how exact they have to be, the bound alone decides.
No kernel may reach another device: no remote copies, remote signals or barrier semaphores. Data moves between devices by JAX's collectives and lax.ppermute only.
A program may use at most 64 MiB of HBM per device.

v0:
```python
import jax
import jax.numpy as jnp
from jax import lax
from jax.sharding import PartitionSpec as P

NSUB = 8
COUPLED = 2
TIME_STEP = 0.25
VISCOSITY = 0.05
COUPLING = 0.5
EXACT_DOT = lax.Precision.HIGHEST


def make_kernels(grid_cells):
    centre = jnp.arange(grid_cells, dtype=jnp.float32) - grid_cells / 2.0 + 0.5
    near_x = (centre / (grid_cells / 16.0))[None, :]
    near_y = (centre / (grid_cells / 16.0))[:, None]
    bell_near = jnp.exp(-(near_x * near_x + near_y * near_y) / 2.0)
    source_x = -near_x * bell_near
    source_y = -near_y * bell_near
    wide_x = (centre / (grid_cells / 8.0))[None, :]
    wide_y = (centre / (grid_cells / 8.0))[:, None]
    bell_wide = jnp.exp(-(wide_x * wide_x + wide_y * wide_y) / 2.0)
    lift_kernel = -wide_x * bell_wide
    drag_kernel = wide_y * bell_wide
    lift_kernel = lift_kernel / jnp.sqrt(jnp.sum(lift_kernel * lift_kernel))
    drag_kernel = drag_kernel / jnp.sqrt(jnp.sum(drag_kernel * drag_kernel))
    return (source_x, source_y, lift_kernel, drag_kernel)


def strip_step(vorticity, flow_x, flow_y, motion, kernels, substeps):
    source_x, source_y, lift_kernel, drag_kernel = kernels
    halves = motion.reshape(motion.shape[0], 2, substeps)
    earlier = jnp.concatenate([jnp.zeros_like(halves[:, :, :1]), halves[:, :, :-1]], axis=2)
    velocity = halves - earlier
    lift_rows = []
    drag_rows = []
    for substep in range(substeps):
        right_cell = jnp.roll(vorticity, -1, axis=2)
        left_cell = jnp.roll(vorticity, 1, axis=2)
        upper_cell = jnp.roll(vorticity, -1, axis=1)
        lower_cell = jnp.roll(vorticity, 1, axis=1)
        laplacian = right_cell + left_cell + upper_cell + lower_cell - 4.0 * vorticity
        tendency = (
            VISCOSITY * laplacian
            - flow_x * (0.5 * (right_cell - left_cell))
            - flow_y * (0.5 * (upper_cell - lower_cell))
        )
        forcing = (
            velocity[:, 0, substep][:, None, None] * source_x
            - velocity[:, 1, substep][:, None, None] * source_y
        )
        vorticity = vorticity + TIME_STEP * tendency + COUPLING * forcing
        lift_rows.append(jnp.sum(vorticity * lift_kernel, axis=(1, 2)))
        drag_rows.append(jnp.sum(vorticity * drag_kernel, axis=(1, 2)))
    return (vorticity, jnp.stack(lift_rows + drag_rows, axis=1))


def apply_block(vectors, matrix):
    return lax.dot_general(vectors, matrix, (((1,), (1,)), ((), ())), precision=EXACT_DOT)


def first_contract(left_side, right_side):
    return lax.dot_general(left_side, right_side, (((0,), (0,)), ((), ())), precision=EXACT_DOT)


def beam_solve(beam_load, pivot_inv, lower_block, upper_block):
    block_count = pivot_inv.shape[0]
    block_size = pivot_inv.shape[1]
    blocks = beam_load.reshape(beam_load.shape[0], block_count, block_size)
    carried = [blocks[:, 0]]
    for block_index in range(1, block_count):
        pivoted = apply_block(carried[-1], pivot_inv[block_index - 1])
        carried.append(blocks[:, block_index] - apply_block(pivoted, lower_block[block_index - 1]))
    solved = [apply_block(carried[-1], pivot_inv[block_count - 1])]
    for block_index in range(block_count - 2, -1, -1):
        remainder = carried[block_index] - apply_block(solved[0], upper_block[block_index])
        solved.insert(0, apply_block(remainder, pivot_inv[block_index]))
    return jnp.concatenate(solved, axis=1)


def local(strip_fields, strip_riser, strip_node, riser_owner, pivot_inv, lower_block, upper_block):
    devices = lax.axis_size("strip")
    position = lax.axis_index("strip")
    per_device = strip_fields.shape[1]
    grid_cells = strip_fields.shape[2]
    node_count = pivot_inv.shape[1] * pivot_inv.shape[2]
    riser_count = riser_owner.shape[1]
    substeps = NSUB
    total_strips = per_device * devices * lax.axis_size("group")
    kernels = make_kernels(grid_cells)
    riser_match = (
        strip_riser[:, 0][:, None] == jnp.arange(riser_count, dtype=jnp.int32)[None, :]
    ).astype(jnp.int32)
    owner_index = jnp.sum(riser_match * riser_owner[0][None, :], axis=1)
    owned_here = owner_index == position
    node_hit = (
        owned_here[:, None]
        & (strip_node[:, None] == jnp.arange(node_count, dtype=jnp.int32)[None, :])
    ).astype(jnp.float32)
    local_owner = lax.dynamic_slice_in_dim(owner_index, position * per_device, per_device)
    local_node = lax.dynamic_slice_in_dim(strip_node, position * per_device, per_device)
    top_taper = 1.0 - jnp.arange(node_count, dtype=jnp.float32) / node_count
    vorticity = strip_fields[0]
    flow_x = strip_fields[1]
    flow_y = strip_fields[2]
    motion = jnp.zeros((per_device, 2 * substeps), jnp.float32)
    displacement = jnp.zeros((2 * substeps, node_count), jnp.float32)
    for coupled_step in range(COUPLED):
        vorticity, force_rows = strip_step(vorticity, flow_x, flow_y, motion, kernels, substeps)
        partial_drag = jnp.sum(force_rows[:, substeps:], axis=0)
        total_drag = lax.psum(partial_drag, ("group", "strip"))
        offset = total_drag / jnp.sqrt(jnp.float32(total_strips))
        beam_load = first_contract(
            lax.all_gather(force_rows, "strip", axis=0, tiled=True), node_hit
        )
        displacement = beam_solve(beam_load, pivot_inv[0], lower_block[0], upper_block[0])
        displacement = displacement.at[substeps:, :].add(offset[:, None] * top_taper[None, :])
        if coupled_step + 1 < COUPLED:
            every_owner = lax.all_gather(displacement[None], "strip", axis=0, tiled=True)
            chosen = jnp.take(every_owner, local_owner, axis=0)
            node_pick = jnp.broadcast_to(local_node[:, None, None], (per_device, 2 * substeps, 1))
            motion = jnp.take_along_axis(chosen, node_pick, axis=2)[:, :, 0]
    return (vorticity, displacement[None])


def solution(mesh):
    in_specs = (
        P(None, ("group", "strip"), None, None),
        P("group", None),
        P("group"),
        P("group", None),
        P(("group", "strip"), None, None, None),
        P(("group", "strip"), None, None, None),
        P(("group", "strip"), None, None, None),
    )
    out_specs = (P(("group", "strip"), None, None), P(("group", "strip"), None, None))
    return jax.shard_map(local, mesh=mesh, in_specs=in_specs, out_specs=out_specs, check_vma=False)
```

profile of v0, /device:TPU:0, one launch (start us, length us, event | category | flops | bytes accessed | tf_op | source)
XLA Modules:
  0.0 231.5 jit_solution(9136430588047142506)
XLA Ops:
  7.2 0.9 slice_bitcast_fusion
  8.5 0.8 copy-done
  12.4 0.7 multiply_reduce_fusion.32
  14.6 0.5 multiply_reduce_fusion.23
  15.9 42.0 %psum.14 = f32[8]{0:T(128)S(1)} all-reduce(f32[8]{0:T(128)S(1)} %reduce_sum.352), channel_id=1, replica_groups=mesh['group'=2,'strip'=16] {'group','strip'}, use_global_device_ids=true, to_apply=%region_20.21 | all-reduce | flops 8 | bytes 64 | tf_op jit(solution)/shard_map/psum | solution.py:112
  58.8 21.0 %all-gather = f32[16,2,16]{2,1,0:T(2,128)S(1)} all-gather(f32[1,2,16]{2,1,0:T(2,128)S(1)} %bitcast.564), channel_id=1, replica_groups=mesh['group'=2,'strip'=16] {'strip'}, dimensions={0}, use_global_device_ids=true | all-gather | bytes 2176 | tf_op jit(solution)/shard_map/all_gather | solution.py:115
  79.8 0.7 copy-done.6
  80.5 0.7 copy-done.5
  81.2 0.2 convolution_bitcast_fusion.1
  81.5 1.0 fusion.167
  82.5 1.1 convolution_subtract_fusion.27
  83.6 1.1 fusion.159
  84.7 1.1 convolution_subtract_fusion.26
  85.8 1.1 fusion.149
  86.9 1.1 convolution_subtract_fusion.25
  88.0 1.1 fusion.139
  89.0 1.1 convolution_subtract_fusion.24
  90.1 1.1 fusion.129
  91.2 1.1 convolution_subtract_fusion.23
  92.2 1.1 fusion.119
  93.3 1.1 convolution_subtract_fusion.22
  94.3 1.1 fusion.109
  95.4 1.1 convolution_subtract_fusion.21
  96.5 1.1 fusion.99
  98.0 0.2 convolution_subtract_fusion.19
  98.2 0.2 fusion.117
  98.4 0.2 convolution_subtract_fusion.18
  98.9 0.2 convolution_subtract_fusion.17
  99.3 0.3 convolution_subtract_fusion.16
  99.8 0.2 convolution_subtract_fusion.15
  100.2 0.3 convolution_subtract_fusion.14
  100.9 0.6 copy-done.3
  102.2 33.8 %all-gather.4.cloned.1.call-done = f32[16,16,1024]{2,1,0:T(8,128)} async-done(((f32[1,16,1024]{2,1,0:T(8,128)}), f32[16,16,1024]{2,1,0:T(8,128)}) %all-gather.4.cloned.1.call-update) | async-done | bytes 1048592 | tf_op jit(solution)/shard_map/all_gather | solution.py:120
  136.0 1.8 gather_fusion
  137.8 0.8 gather_fusion.1
  142.2 1.1 multiply_reduce_fusion.7
  144.2 38.9 %psum.15 = f32[8]{0:T(128)S(1)} all-reduce(f32[8]{0:T(128)S(1)} %reduce_sum.369), channel_id=1, replica_groups=mesh['group'=2,'strip'=16] {'group','strip'}, use_global_device_ids=true, to_apply=%region_38.39 | all-reduce | flops 8 | bytes 64 | tf_op jit(solution)/shard_map/psum | solution.py:112
  183.9 20.6 %all-gather.1 = f32[16,2,16]{2,1,0:T(2,128)S(1)} all-gather(f32[1,2,16]{2,1,0:T(2,128)S(1)} %bitcast.565), channel_id=1, replica_groups=mesh['group'=2,'strip'=16] {'strip'}, dimensions={0}, use_global_device_ids=true | all-gather | bytes 2176 | tf_op jit(solution)/shard_map/all_gather | solution.py:115
  204.5 0.2 convolution_bitcast_fusion
  204.8 1.0 fusion.164
  205.8 1.1 convolution_subtract_fusion.13
  206.9 1.1 fusion.155
  208.0 1.1 convolution_subtract_fusion.12
  209.0 1.1 fusion.145
  210.1 1.1 convolution_subtract_fusion.11
  211.2 1.1 fusion.135
  212.2 1.1 convolution_subtract_fusion.10
  213.3 1.1 fusion.125
  214.3 1.1 convolution_subtract_fusion.9
  215.4 1.1 fusion.115
  216.5 1.1 convolution_subtract_fusion.8
  217.5 1.1 fusion.105
  218.6 1.1 convolution_subtract_fusion.7
  219.6 1.1 fusion.97
  220.7 0.2 convolution_subtract_fusion.6
  220.9 0.2 fusion.103
  221.2 0.2 convolution_subtract_fusion.5
  221.4 0.2 fusion.113
  221.6 0.2 convolution_subtract_fusion.4
  222.1 0.2 convolution_subtract_fusion.3
  222.5 0.2 convolution_subtract_fusion.2
  223.0 0.2 convolution_subtract_fusion.1
  223.4 0.2 convolution_subtract_fusion
  224.1 0.6 copy-done.4
  (188 shorter events, 13.7 us)
Async XLA Ops:
  7.2 128.8 %all-gather.4.cloned.1.call-start = ((), (), s32[]{:S(2)}) async-start(), calls=%async_computation | async-start | bytes 1114112 | tf_op jit(solution)/shard_map/all_gather | solution.py:120
  8.3 1.0 copy-start
  79.8 0.7 copy-start.6
  79.8 0.7 copy-start.7
  80.5 0.7 copy-start.5
  84.7 12.9 %copy-start.2 = (f32[1,7,128,128]{3,2,1,0:T(8,128)S(1)}, f32[1,7,128,128]{3,2,1,0:T(8,128)}, u32[]{:S(2)}) copy-start(f32[1,7,128,128]{3,2,1,0:T(8,128)} %param.17) | copy-start | bytes 1376260
  85.8 12.0 %copy-start.1 = (f32[1,8,128,128]{3,2,1,0:T(8,128)S(1)}, f32[1,8,128,128]{3,2,1,0:T(8,128)}, u32[]{:S(2)}) copy-start(f32[1,8,128,128]{3,2,1,0:T(8,128)} %param.15) | copy-start | bytes 1572868
  100.9 0.6 copy-start.3
  224.1 0.6 copy-start.4
Sparse Core Ops, SparseCore 0:
  101.7 34.2 all-gather.3
where the time goes:
time: 233 us; the launch traced here: 232 us
  blocking collectives  123 us (53%)
  matrix products  38.5 us (17%)
  waiting for transfers between devices  33.8 us (15%)
  between operations  16.3 us (7%)
  local copies, waits for them, and re-layouts  14.4 us (6%)
  other arithmetic  5.94 us (3%)
    psum x2, blocking collectives, local(): total_drag = lax.psum(partial_drag, ('group', 'strip'))  80.9 us
    all_gather x2, blocking collectives, local(): lax.all_gather(force_rows, 'strip', axis=0, tiled=True)  41.6 us
    dot_general x58, matrix products, apply_block(): lax.dot_general(vectors, matrix, (((1,), (1,)), ((), ())), precision=EXAC...  38 us
    all_gather x1, waiting for transfers between devices, local(): lax.all_gather(displacement[None], 'strip', axis=0, tiled=True)  33.8 us
  transfers between devices with their start and end apart: 1, of which 1 were waited for; matrix products, arithmetic and copies ran while one was open for 0% of the time, Pallas kernels for 0%

commit v1 on v0

--- a/solution.py
+++ b/solution.py
@@ -9,6 +9,28 @@
 VISCOSITY = 0.05
 COUPLING = 0.5
 EXACT_DOT = lax.Precision.HIGHEST
+
+
+def laid_out(tiles, dim):
+    tiles = jnp.moveaxis(tiles, 0, dim)
+    dims = tiles.shape
+    return tiles.reshape(*dims[:dim], dims[dim] * dims[dim + 1], *dims[dim + 2 :])
+
+
+def grow_blocks(x, axis):
+    size = lax.axis_size(axis)
+    parts = x[None]
+    for level in range(size.bit_length() - 1):
+        stride = 1 << level
+        partner_block = lax.ppermute(parts, axis, [(i, i ^ stride) for i in range(size)])
+        both = jnp.stack([parts, partner_block])
+        upper = lax.axis_index(axis) >> level & 1
+        parts = jnp.where(upper == 0, both, both[::-1]).reshape(-1, *x.shape)
+    return parts
+
+
+def gather_by_bits(value, axis, dim):
+    return laid_out(grow_blocks(value, axis), dim)
 
 
 def make_kernels(grid_cells):
@@ -111,9 +133,7 @@
         partial_drag = jnp.sum(force_rows[:, substeps:], axis=0)
         total_drag = lax.psum(partial_drag, ("group", "strip"))
         offset = total_drag / jnp.sqrt(jnp.float32(total_strips))
-        beam_load = first_contract(
-            lax.all_gather(force_rows, "strip", axis=0, tiled=True), node_hit
-        )
+        beam_load = first_contract(gather_by_bits(force_rows, "strip", 0), node_hit)
         displacement = beam_solve(beam_load, pivot_inv[0], lower_block[0], upper_block[0])
         displacement = displacement.at[substeps:, :].add(offset[:, None] * top_taper[None, :])
         if coupled_step + 1 < COUPLED:

time: 233 us -> 190 us (0.82)
  blocking collectives: 123 us -> 81 us
  matrix products: 38.5 us -> 13.4 us
  waiting for transfers between devices: 33.8 us -> 50.1 us
  starting transfers between devices: 0.04 us -> 9.73 us
    all_gather x2 -> x0, blocking collectives: 41.6 us -> none  [local(): lax.all_gather(force_rows, 'strip', axis=0, tiled=True)]
    dot_general x58, matrix products: 38 us -> 12.9 us  [apply_block(): lax.dot_general(vectors, matrix, (((1,), (1,)), ((), ())), precision=EXAC...]
    ppermute x0 -> x8, waiting for transfers between devices: none -> 13 us  [grow_blocks(): lax.ppermute(parts, axis, [(i, i ^ stride) for i in range(size)])]
    ppermute x0 -> x8, starting transfers between devices: none -> 9.69 us  [grow_blocks(): lax.ppermute(parts, axis, [(i, i ^ stride) for i in range(size)])]
    all_gather x1, waiting for transfers between devices: 33.8 us -> 37 us  [local(): lax.all_gather(displacement[None], 'strip', axis=0, tiled=True)]
  transfers between devices with their start and end apart: 1 -> 9, of which waited for: 1 -> 7; matrix products, arithmetic and copies ran while one was open for 0% -> 0% of each run, Pallas kernels for 0% -> 0%
where the time goes in v1:
time: 190 us; the launch traced here: 189 us
  blocking collectives  81 us (43%)
  waiting for transfers between devices  50.1 us (26%)
  between operations  16.3 us (9%)
  matrix products  13.4 us (7%)
  local copies, waits for them, and re-layouts  12.9 us (7%)
  starting transfers between devices  9.73 us (5%)
  other arithmetic  5.99 us (3%)
    psum x2, blocking collectives, local(): total_drag = lax.psum(partial_drag, ('group', 'strip'))  81 us
    all_gather x1, waiting for transfers between devices, local(): lax.all_gather(displacement[None], 'strip', axis=0, tiled=True)  37 us
    ppermute x8, waiting for transfers between devices, grow_blocks(): lax.ppermute(parts, axis, [(i, i ^ stride) for i in range(size)])  13 us
    dot_general x58, matrix products, apply_block(): lax.dot_general(vectors, matrix, (((1,), (1,)), ((), ())), precision=EXAC...  12.9 us
    ppermute x8, starting transfers between devices, grow_blocks(): lax.ppermute(parts, axis, [(i, i ^ stride) for i in range(size)])  9.69 us
  transfers between devices with their start and end apart: 9, of which 7 were waited for; matrix products, arithmetic and copies ran while one was open for 0% of the time, Pallas kernels for 0%

profile of v1, /device:TPU:0, one launch (start us, length us, event | category | flops | bytes accessed | tf_op | source)
XLA Modules:
  0.0 189.5 jit_solution(10542166249154968222)
XLA Ops:
  7.2 0.9 slice_bitcast_fusion
  8.5 0.8 copy-done
  12.3 0.7 multiply_reduce_fusion.32
  14.6 0.5 multiply_reduce_fusion.23
  16.6 0.5 collective-permute-start
  17.3 41.6 %psum.14 = f32[8]{0:T(128)S(1)} all-reduce(f32[8]{0:T(128)S(1)} %reduce_sum.352), channel_id=1, replica_groups=mesh['group'=2,'strip'=16] {'group','strip'}, use_global_device_ids=true, to_apply=%region_20.21 | all-reduce | flops 8 | bytes 64 | tf_op jit(solution)/shard_map/psum | solution.py:134
  59.0 2.3 %collective-permute-start.1 = (f32[2,2,16]{2,1,0:T(2,128)S(1)}, f32[2,2,16]{2,1,0:T(2,128)S(1)}, u32[]{:S(2)}, u32[]{:S(2)}) collective-permute-start(f32[2,2,16]{2,1,0:T(2,128)S(1)} %get-tuple-element.325), channel_id=1, source_target_pairs={{0,2},{1,3},{2,0},{3,1},{4,6},{5,7},{6,4},{7,5},{8,10},{9,11},{10,... | collective-permute-start | bytes 776 | tf_op jit(solution)/shard_map/ppermute | solution.py:25
  61.3 1.6 collective-permute-done.1
  62.9 1.6 collective-permute-start.2
  64.5 2.1 %collective-permute-done.2 = f32[4,2,16]{2,1,0:T(2,128)S(1)} collective-permute-done((f32[4,2,16]{2,1,0:T(2,128)S(1)}, f32[4,2,16]{2,1,0:T(2,128)S(1)}, u32[]{:S(2)}, u32[]{:S(2)}) %collective-permute-start.2) | collective-permute-done | bytes 544 | tf_op jit(solution)/shard_map/ppermute | solution.py:25
  66.6 2.4 %collective-permute-start.3 = (f32[8,2,16]{2,1,0:T(2,128)S(1)}, f32[8,2,16]{2,1,0:T(2,128)S(1)}, u32[]{:S(2)}, u32[]{:S(2)}) collective-permute-start(f32[8,2,16]{2,1,0:T(2,128)S(1)} %bitcast.581), channel_id=1, source_target_pairs={{0,8},{1,9},{2,10},{3,11},{4,12},{5,13},{6,14},{7,15},{8,0},{9,1},... | collective-permute-start | bytes 3080 | tf_op jit(solution)/shard_map/ppermute | solution.py:25
  69.0 2.2 %collective-permute-done.3 = f32[8,2,16]{2,1,0:T(2,128)S(1)} collective-permute-done((f32[8,2,16]{2,1,0:T(2,128)S(1)}, f32[8,2,16]{2,1,0:T(2,128)S(1)}, u32[]{:S(2)}, u32[]{:S(2)}) %collective-permute-start.3) | collective-permute-done | bytes 1056 | tf_op jit(solution)/shard_map/ppermute | solution.py:25
  71.2 0.2 fusion.81
  72.1 0.2 convolution_subtract_fusion.26
  72.6 0.2 convolution_subtract_fusion.25
  73.0 0.2 convolution_subtract_fusion.24
  73.5 0.2 convolution_subtract_fusion.23
  73.7 0.2 fusion.118
  73.9 0.2 convolution_subtract_fusion.22
  74.1 0.2 fusion.108
  74.4 0.2 convolution_subtract_fusion.21
  74.6 0.2 fusion.98
  75.1 0.2 fusion.106
  75.3 0.2 convolution_subtract_fusion.19
  75.5 0.2 fusion.116
  75.7 0.3 convolution_subtract_fusion.18
  76.2 0.2 convolution_subtract_fusion.17
  76.4 0.2 fusion.136
  76.6 0.3 convolution_subtract_fusion.16
  77.3 0.2 fusion.156
  77.5 0.3 convolution_subtract_fusion.14
  77.8 0.2 convolution_dynamic-update-slice_fusion.1
  78.2 0.6 copy-done.4
  79.4 37.0 %all-gather.2.cloned.1.call-done = f32[16,16,1024]{2,1,0:T(8,128)} async-done(((f32[1,16,1024]{2,1,0:T(8,128)}), f32[16,16,1024]{2,1,0:T(8,128)}) %all-gather.2.cloned.1.call-update) | async-done | bytes 1048592 | tf_op jit(solution)/shard_map/all_gather | solution.py:140
  116.5 1.8 gather_fusion
  118.4 0.8 gather_fusion.1
  122.7 1.1 multiply_reduce_fusion.7
  125.4 0.3 collective-permute-start.4
  125.7 0.9 collective-permute-done.4
  126.6 0.6 collective-permute-start.5
  127.2 3.1 %collective-permute-done.5 = f32[2,2,16]{2,1,0:T(2,128)S(1)} collective-permute-done((f32[2,2,16]{2,1,0:T(2,128)S(1)}, f32[2,2,16]{2,1,0:T(2,128)S(1)}, u32[]{:S(2)}, u32[]{:S(2)}) %collective-permute-start.5) | collective-permute-done | bytes 288 | tf_op jit(solution)/shard_map/ppermute | solution.py:25
  130.3 0.6 collective-permute-start.6
  131.0 39.4 %psum.15 = f32[8]{0:T(128)S(1)} all-reduce(f32[8]{0:T(128)S(1)} %reduce_sum.369), channel_id=1, replica_groups=mesh['group'=2,'strip'=16] {'group','strip'}, use_global_device_ids=true, to_apply=%region_38.39 | all-reduce | flops 8 | bytes 64 | tf_op jit(solution)/shard_map/psum | solution.py:134
  170.4 1.4 collective-permute-start.7
  171.8 3.2 %collective-permute-done.7 = f32[8,2,16]{2,1,0:T(2,128)S(1)} collective-permute-done((f32[8,2,16]{2,1,0:T(2,128)S(1)}, f32[8,2,16]{2,1,0:T(2,128)S(1)}, u32[]{:S(2)}, u32[]{:S(2)}) %collective-permute-start.7) | collective-permute-done | bytes 1056 | tf_op jit(solution)/shard_map/ppermute | solution.py:25
  175.1 0.2 fusion.80
  175.5 0.2 convolution_subtract_fusion.13
  175.9 0.2 convolution_subtract_fusion.12
  176.4 0.2 convolution_subtract_fusion.11
  176.8 0.2 convolution_subtract_fusion.10
  177.3 0.2 convolution_subtract_fusion.9
  177.5 0.2 fusion.114
  177.7 0.2 convolution_subtract_fusion.8
  178.0 0.2 fusion.104
  178.2 0.2 convolution_subtract_fusion.7
  178.4 0.2 fusion.96
  178.6 0.2 convolution_subtract_fusion.6
  179.1 0.2 convolution_subtract_fusion.5
  179.5 0.2 convolution_subtract_fusion.4
  180.0 0.2 convolution_subtract_fusion.3
  180.4 0.2 convolution_subtract_fusion.2
  180.9 0.2 convolution_subtract_fusion.1
  181.3 0.2 convolution_subtract_fusion
  182.0 0.6 copy-done.5
  (217 shorter events, 15.8 us)
Async XLA Ops:
  7.2 109.3 %all-gather.2.cloned.1.call-start = ((), (), s32[]{:S(2)}) async-start(), calls=%async_computation | async-start | bytes 1114112 | tf_op jit(solution)/shard_map/all_gather | solution.py:140
  8.3 1.0 copy-start
  14.5 44.3 %copy-start.7 = (s32[1,4]{1,0:T(1,128)S(1)}, s32[1,4]{1,0:T(1,128)}, u32[]{:S(2)}) copy-start(s32[1,4]{1,0:T(1,128)} %param.14) | copy-start | bytes 52
  14.5 44.3 %copy-start.8 = (s32[32,1]{0,1:T(1,128)S(1)}, s32[32,1]{0,1:T(1,128)}, u32[]{:S(2)}) copy-start(s32[32,1]{0,1:T(1,128)} %param.12) | copy-start | bytes 388
  14.6 56.7 %copy-start.6 = (s32[32]{0:T(128)S(1)}, s32[32]{0:T(128)}, u32[]{:S(2)}) copy-start(s32[32]{0:T(128)} %param.13) | copy-start | bytes 388
  14.6 56.9 %copy-start.1 = (f32[1,8,128,128]{3,2,1,0:T(8,128)S(1)}, f32[1,8,128,128]{3,2,1,0:T(8,128)}, u32[]{:S(2)}) copy-start(f32[1,8,128,128]{3,2,1,0:T(8,128)} %param.15) | copy-start | bytes 1572868
  15.0 56.6 %copy-start.2 = (f32[1,7,128,128]{3,2,1,0:T(8,128)S(1)}, f32[1,7,128,128]{3,2,1,0:T(8,128)}, u32[]{:S(2)}) copy-start(f32[1,7,128,128]{3,2,1,0:T(8,128)} %param.16) | copy-start | bytes 1376260
  16.6 42.3 %collective-permute-start = (f32[1,2,16]{2,1,0:T(2,128)S(1)}, f32[1,2,16]{2,1,0:T(2,128)S(1)}, u32[]{:S(2)}, u32[]{:S(2)}) collective-permute-start(f32[1,2,16]{2,1,0:T(2,128)S(1)} %bitcast.594), channel_id=1, source_target_pairs={{0,1},{1,0},{2,3},{3,2},{4,5},{5,4},{6,7},{7,6},{8,9},{9,8},{10,11... | collective-permute-start | bytes 392 | tf_op jit(solution)/shard_map/ppermute | solution.py:25
  59.0 3.9 %collective-permute-start.1 = (f32[2,2,16]{2,1,0:T(2,128)S(1)}, f32[2,2,16]{2,1,0:T(2,128)S(1)}, u32[]{:S(2)}, u32[]{:S(2)}) collective-permute-start(f32[2,2,16]{2,1,0:T(2,128)S(1)} %get-tuple-element.325), channel_id=1, source_target_pairs={{0,2},{1,3},{2,0},{3,1},{4,6},{5,7},{6,4},{7,5},{8,10},{9,11},{10,... | collective-permute-start | bytes 776 | tf_op jit(solution)/shard_map/ppermute | solution.py:25
  62.9 3.7 %collective-permute-start.2 = (f32[4,2,16]{2,1,0:T(2,128)S(1)}, f32[4,2,16]{2,1,0:T(2,128)S(1)}, u32[]{:S(2)}, u32[]{:S(2)}) collective-permute-start(f32[4,2,16]{2,1,0:T(2,128)S(1)} %bitcast.589), channel_id=1, source_target_pairs={{0,4},{1,5},{2,6},{3,7},{4,0},{5,1},{6,2},{7,3},{8,12},{9,13},{10,... | collective-permute-start | bytes 1544 | tf_op jit(solution)/shard_map/ppermute | solution.py:25
  66.6 4.6 %collective-permute-start.3 = (f32[8,2,16]{2,1,0:T(2,128)S(1)}, f32[8,2,16]{2,1,0:T(2,128)S(1)}, u32[]{:S(2)}, u32[]{:S(2)}) collective-permute-start(f32[8,2,16]{2,1,0:T(2,128)S(1)} %bitcast.581), channel_id=1, source_target_pairs={{0,8},{1,9},{2,10},{3,11},{4,12},{5,13},{6,14},{7,15},{8,0},{9,1},... | collective-permute-start | bytes 3080 | tf_op jit(solution)/shard_map/ppermute | solution.py:25
  72.3 2.5 %copy-start.3 = (f32[1,7,128,128]{3,2,1,0:T(8,128)S(1)}, f32[1,7,128,128]{3,2,1,0:T(8,128)}, u32[]{:S(2)}) copy-start(f32[1,7,128,128]{3,2,1,0:T(8,128)} %param.17) | copy-start | bytes 1376260
  78.2 0.6 copy-start.4
  125.4 1.2 collective-permute-start.4
  126.6 3.6 %collective-permute-start.5 = (f32[2,2,16]{2,1,0:T(2,128)S(1)}, f32[2,2,16]{2,1,0:T(2,128)S(1)}, u32[]{:S(2)}, u32[]{:S(2)}) collective-permute-start(f32[2,2,16]{2,1,0:T(2,128)S(1)} %get-tuple-element.323), channel_id=1, source_target_pairs={{0,2},{1,3},{2,0},{3,1},{4,6},{5,7},{6,4},{7,5},{8,10},{9,11},{10,... | collective-permute-start | bytes 776 | tf_op jit(solution)/shard_map/ppermute | solution.py:25
  130.3 40.1 %collective-permute-start.6 = (f32[4,2,16]{2,1,0:T(2,128)S(1)}, f32[4,2,16]{2,1,0:T(2,128)S(1)}, u32[]{:S(2)}, u32[]{:S(2)}) collective-permute-start(f32[4,2,16]{2,1,0:T(2,128)S(1)} %bitcast.587), channel_id=1, source_target_pairs={{0,4},{1,5},{2,6},{3,7},{4,0},{5,1},{6,2},{7,3},{8,12},{9,13},{10,... | collective-permute-start | bytes 1544 | tf_op jit(solution)/shard_map/ppermute | solution.py:25
  170.4 4.6 %collective-permute-start.7 = (f32[8,2,16]{2,1,0:T(2,128)S(1)}, f32[8,2,16]{2,1,0:T(2,128)S(1)}, u32[]{:S(2)}, u32[]{:S(2)}) collective-permute-start(f32[8,2,16]{2,1,0:T(2,128)S(1)} %bitcast.583), channel_id=1, source_target_pairs={{0,8},{1,9},{2,10},{3,11},{4,12},{5,13},{6,14},{7,15},{8,0},{9,1},... | collective-permute-start | bytes 3080 | tf_op jit(solution)/shard_map/ppermute | solution.py:25
  182.0 0.6 copy-start.5
Sparse Core Ops, SparseCore 0:
  79.0 37.4 all-gather.1
